TPU v7x, 256 devices: a whole 4x4x8 slice. The times are simulated.
256 devices in a mesh: wide: 32 (over x, y, core), blk: 8 (over z).
Axes of the slice: x: 4, y: 4, z: 8, core: 2. Of those that a mesh axis runs over, the one named last changes fastest.
Arguments:
- tokens: bfloat16 [1024, 8192], P('wide', 'blk'), may hold values from -6 to 6
- target: bfloat16 [1024, 8192], P('wide', 'blk'), may hold values from -3 to 3
- probe_vector: float32 [8192], P('blk'), may hold values from -12 to 12
- weight_in: bfloat16 [256, 8, 2, 128, 128], P('wide', 'blk'), may hold values from -0.375 to 0.375
- weight_out: bfloat16 [256, 8, 2, 128, 128], P('wide', 'blk'), may hold values from -0.09375 to 0.09375
- slot_rows: int32 [256, 8, 2], P('wide', 'blk'), may hold values from 0 to 7, as said below
- slot_count: int32 [256, 8], P('wide', 'blk'), may hold values from 0 to 2, as said below
Outputs:
- outputs: bfloat16 [1024, 8192], P('wide', 'blk')
- token_grad: bfloat16 [1024, 8192], P('wide', 'blk')
- grad_in: float32 [256, 8, 2, 128, 128], P('wide', 'blk')
- grad_out: float32 [256, 8, 2, 128, 128], P('wide', 'blk')
Inputs may be any that keep to these rules, and one draw needn't show every extreme that they name: `slot_rows`: the 2 entries of one (j, g) are distinct feature blocks of the row group. `slot_count`: every hidden block column has 2 used slots in at least one row group.
All inputs are finite; a program needn't handle non-finite values.
Results may differ from a plain program's by a relative error of at most 0.033.
Values may be sent and summed in bfloat16 or wider, within the bound.
No kernel may reach another device: no remote copies, remote signals or barrier semaphores. Data moves between devices by JAX's collectives and lax.ppermute only.
A program may use at most 64 MiB of HBM per device.

v0:
```python
import math
import jax
import jax.numpy as jnp
from jax import lax
from jax.sharding import PartitionSpec as P


def activate(value):
    return jax.nn.gelu(value, approximate=True)


def activate_slope(value):
    return jax.jvp(activate, (value,), (jnp.ones_like(value),))[1]


def row_stride(count, limit):
    return math.gcd(count, limit)


def by_blocks(blockfn, row_count, limit):
    stride = row_stride(row_count, limit)
    pieces = lax.map(
        lambda index: blockfn(index * stride, stride),
        jnp.arange(row_count // stride, dtype=jnp.int32),
    )
    return pieces.reshape((row_count,) + pieces.shape[2:])


def pick_rows(activity, row_index, block):
    row_total = activity.shape[0]
    columns, slots = row_index.shape
    blocks = activity.reshape(row_total, activity.shape[1] // block, block)
    return jnp.take(blocks, row_index.reshape(-1), axis=1).reshape(row_total, columns, slots, block)


def body(tokens, target, probe_vector, weight_in, weight_out, slot_rows, slot_count):
    columns, unit, slots, block, width_two = weight_in.shape
    features = tokens.shape[1]
    feature_blocks = features // block
    row_index = slot_rows[:, 0]
    in_use = lax.broadcasted_iota(jnp.int32, (columns, slots), 1) < slot_count[:, 0][:, None]
    mask_low = in_use.astype(jnp.bfloat16)[:, :, None, None]
    mask_full = in_use.astype(jnp.float32)[:, :, None, None]
    tiles_in = weight_in[:, 0] * mask_low
    tiles_out = weight_out[:, 0] * mask_low
    onehot = (
        row_index[:, :, None]
        == lax.broadcasted_iota(jnp.int32, (columns, slots, feature_blocks), 2)
    ).astype(jnp.float32)
    chosen = jnp.take(
        probe_vector.reshape(feature_blocks, block), row_index.reshape(-1), axis=0
    ).reshape(columns, slots, block)
    image_part = jnp.einsum(
        "jsk,jskn->jn", chosen, tiles_in.astype(jnp.float32), precision=lax.Precision.HIGHEST
    )
    image, norm_probe = lax.psum((image_part, jnp.sum(probe_vector * probe_vector)), "blk")
    norm_image = lax.psum(jnp.sum(image * image), "wide")
    spectral = jnp.sqrt(norm_image / norm_probe)
    x_full = lax.all_gather(tokens, "wide", axis=0, tiled=True)
    all_rows = x_full.shape[0]
    block_rows = all_rows // lax.axis_size("blk")
    owned = tokens.shape[0]

    def hidden_block_term(start_row, count):
        picked = pick_rows(lax.dynamic_slice_in_dim(x_full, start_row, count, 0), row_index, block)
        product = jnp.einsum("tjsk,jskn->tjn", picked, tiles_in, preferred_element_type=jnp.float32)
        return product.reshape(count, columns * block)

    hidden_own = (
        lax.psum_scatter(
            by_blocks(hidden_block_term, block_rows * lax.axis_size("blk"), 512).astype(
                jnp.bfloat16
            ),
            "blk",
            scatter_dimension=0,
            tiled=True,
        ).astype(jnp.float32)
        / spectral
    )
    active_own = activate(hidden_own).astype(jnp.bfloat16)
    active_full = lax.all_gather(active_own, "blk", axis=0, tiled=True)

    def output_block_term(start_row, count):
        active = lax.dynamic_slice_in_dim(active_full, start_row, count, 0).reshape(
            count, columns, block
        )
        contrib = jnp.einsum(
            "tjk,jskn->tjsn", active, tiles_out, preferred_element_type=jnp.float32
        )
        return jnp.einsum("tjsn,jsr->trn", contrib, onehot).reshape(count, features)

    outputs = lax.psum_scatter(
        by_blocks(output_block_term, owned * lax.axis_size("wide"), 256).astype(jnp.bfloat16),
        "wide",
        scatter_dimension=0,
        tiled=True,
    )
    residual = (outputs.astype(jnp.float32) - target.astype(jnp.float32)).astype(jnp.bfloat16)
    error_full = lax.all_gather(residual, "wide", axis=0, tiled=True)

    def back_block_term(start_row, count):
        picked = pick_rows(
            lax.dynamic_slice_in_dim(error_full, start_row, count, 0), row_index, block
        )
        product = jnp.einsum(
            "tjsn,jskn->tjk", picked, tiles_out, preferred_element_type=jnp.float32
        )
        return product.reshape(count, columns * block)

    back_own = lax.psum_scatter(
        by_blocks(back_block_term, block_rows * lax.axis_size("blk"), 512).astype(jnp.bfloat16),
        "blk",
        scatter_dimension=0,
        tiled=True,
    ).astype(jnp.float32)
    slope_own = (back_own * activate_slope(hidden_own)).astype(jnp.bfloat16)
    slope_full = lax.all_gather(slope_own, "blk", axis=0, tiled=True)
    stride = row_stride(all_rows, 256)

    def grads_block(index, totals):
        start_row = index * stride
        picked_in = pick_rows(
            lax.dynamic_slice_in_dim(x_full, start_row, stride, 0), row_index, block
        )
        picked_err = pick_rows(
            lax.dynamic_slice_in_dim(error_full, start_row, stride, 0), row_index, block
        )
        slope = lax.dynamic_slice_in_dim(slope_full, start_row, stride, 0).reshape(
            stride, columns, block
        )
        active = lax.dynamic_slice_in_dim(active_full, start_row, stride, 0).reshape(
            stride, columns, block
        )
        part_in = jnp.einsum("tjsk,tjn->jskn", picked_in, slope, preferred_element_type=jnp.float32)
        part_out = jnp.einsum(
            "tjk,tjsn->jskn", active, picked_err, preferred_element_type=jnp.float32
        )
        return (totals[0] + part_in, totals[1] + part_out)

    empty = jnp.zeros((columns, slots, block, block), jnp.float32)
    raw_in, raw_out = lax.fori_loop(0, all_rows // stride, grads_block, (empty, empty))
    raw_in = raw_in * mask_full
    grad_out = raw_out * mask_full
    curvature = lax.psum(jnp.sum(raw_in * tiles_in.astype(jnp.float32)), ("wide", "blk"))
    outer = jnp.einsum("jsk,jn->jskn", chosen, image) * mask_full
    grad_in = raw_in / spectral - curvature / (spectral**3 * norm_probe) * outer

    def input_block_term(start_row, count):
        slope = lax.dynamic_slice_in_dim(slope_full, start_row, count, 0).reshape(
            count, columns, block
        )
        contrib = jnp.einsum("tjn,jskn->tjsk", slope, tiles_in, preferred_element_type=jnp.float32)
        return jnp.einsum("tjsk,jsr->trk", contrib, onehot).reshape(count, features)

    token_grad = (
        lax.psum_scatter(
            by_blocks(input_block_term, owned * lax.axis_size("wide"), 256).astype(jnp.bfloat16),
            "wide",
            scatter_dimension=0,
            tiled=True,
        ).astype(jnp.float32)
        / spectral
    ).astype(jnp.bfloat16)
    return (outputs, token_grad, grad_in[:, None], grad_out[:, None])


def solution(mesh):
    in_specs = (
        P("wide", "blk"),
        P("wide", "blk"),
        P("blk"),
        P("wide", "blk", None, None, None),
        P("wide", "blk", None, None, None),
        P("wide", "blk", None),
        P("wide", "blk"),
    )
    out_specs = (
        P("wide", "blk"),
        P("wide", "blk"),
        P("wide", "blk", None, None, None),
        P("wide", "blk", None, None, None),
    )
    return jax.shard_map(body, mesh=mesh, in_specs=in_specs, out_specs=out_specs, check_vma=False)
```

profile of v0, /device:TPU:1, one launch (start us, length us, event | category | flops | bytes accessed | tf_op | source)
XLA Modules:
  0.0 652.1 jit_solution(13190907771488800029)
XLA Ops:
  9.5 2.1 bitcast_multiply_fusion
  12.7 51.0 %all-gather.5.cloned.1.call-done = bf16[1024,1024]{1,0:T(8,128)(2,1)} async-done(((bf16[32,1024]{1,0:T(8,128)(2,1)}), bf16[1024,1024]{1,0:T(8,128)(2,1)}) %all-gather.5.cloned.1.call-update) | async-done | bytes 2097168 | tf_op jit(solution)/shard_map/all_gather | solution.py:59
  63.7 3.9 copy.95
  67.6 1.5 broadcast.110.clone
  69.1 15.2 %while.63 = (s32[]{:T(128)}, bf16[2,512,1024]{1,2,0:T(8,128)(2,1)}, s32[2]{0:T(128)S(1)}, bf16[1024,1024]{0,1:T(8,128)(2,1)}, s32[8,1,2]{2,0,1:T(8,128)}, /*inde...) while((s32[]{:T(128)}, bf16[2,512,1024]{1,2,0:T(8,128)(2,1)}, ...), condition=%wide.wide.region_1.3_spmd, body=%wide.wide.region_0.0_spmd.sunk | while | flops 269485216 | bytes 37229152 | solution.py:22
  70.3 1.3 constant_dynamic-slice_fusion.20
  75.3 1.3 copy-done.11
  82.9 1.3 copy-done.11
  84.3 3.9 copy.132
  90.7 15.5 %all-reduce = (f32[8,128]{1,0:T(8,128)S(1)}, f32[]{:T(128)}) all-reduce(f32[8,128]{1,0:T(8,128)S(1)} %bitcast.244, f32[]{:T(128)} %multiply_reduce_fusion.1), channel_id=1, replica_groups=mesh['wide'=32,'blk'=8] {'blk'}, use_global_device_ids=true, to_apply=%region_3.5 | all-reduce | flops 1025 | bytes 8200 | tf_op jit(solution)/shard_map/psum | solution.py:56
  106.8 65.7 %psum.29 = f32[]{:T(128)} all-reduce(f32[]{:T(128)} %multiply_reduce_fusion.2), channel_id=1, replica_groups=mesh['wide'=32,'blk'=8] {'wide'}, use_global_device_ids=true, to_apply=%region_5.7 | all-reduce | flops 1 | bytes 8 | tf_op jit(solution)/shard_map/psum | solution.py:57
  176.0 37.4 %all-gather.7.cloned.1.call-done = bf16[1024,1024]{0,1:T(8,128)(2,1)} async-done(((bf16[128,1024]{0,1:T(8,128)(2,1)}), bf16[1024,1024]{0,1:T(8,128)(2,1)}) %all-gather.7.cloned.1.call-update) | async-done | bytes 2097168 | tf_op jit(solution)/shard_map/all_gather | solution.py:81
  213.4 1.6 broadcast.109.clone
  215.0 18.3 %while.61 = (s32[]{:T(128)}, bf16[4,256,1024]{2,1,0:T(8,128)(2,1)}, s32[4]{0:T(128)S(1)}, bf16[1024,1024]{0,1:T(8,128)(2,1)}, bf16[8,2,128,128]{3,2,1,0:T(8,128)...) while((s32[]{:T(128)}, bf16[4,256,1024]{2,1,0:T(8,128)(2,1)}, ...), condition=%wide.region_9.11_spmd.clone, body=%wide.region_8.10_spmd.clone.sunk | while | flops 142606592 | bytes 6816483 | solution.py:22
  233.4 87.8 %reduce-scatter.9.cloned.1.call-done = bf16[32,1024]{1,0:T(8,128)(2,1)} async-done(((bf16[1024,1024]{1,0:T(8,128)(2,1)}), bf16[32,1024]{1,0:T(8,128)(2,1)}) %reduce-scatter.9.cloned.1.call-update) | async-done | bytes 65552 | tf_op jit(solution)/shard_map/reduce_scatter | solution.py:92
  321.3 1.5 subtract_convert_fusion
  322.9 51.6 %all-gather.9.cloned.1.call-done = bf16[1024,1024]{1,0:T(8,128)(2,1)} async-done(((bf16[32,1024]{1,0:T(8,128)(2,1)}), bf16[1024,1024]{1,0:T(8,128)(2,1)}) %all-gather.9.cloned.1.call-update) | async-done | bytes 2097168 | tf_op jit(solution)/shard_map/all_gather | solution.py:99
  374.5 3.9 copy.101
  378.5 1.5 broadcast.110
  380.0 15.5 %while.64 = (s32[]{:T(128)}, bf16[2,512,1024]{1,2,0:T(8,128)(2,1)}, s32[2]{0:T(128)S(1)}, bf16[1024,1024]{0,1:T(8,128)(2,1)}, s32[8,1,2]{2,0,1:T(8,128)}, /*inde...) while((s32[]{:T(128)}, bf16[2,512,1024]{1,2,0:T(8,128)(2,1)}, ...), condition=%wide.wide.region_12.14_spmd, body=%wide.wide.region_11.13_spmd.sunk | while | flops 269485216 | bytes 39326336 | solution.py:22
  386.4 1.4 copy-done.13
  394.1 1.4 copy-done.13
  395.5 4.0 copy.133
  399.5 37.0 %reduce-scatter.15.cloned.1.call-done = bf16[128,1024]{1,0:T(8,128)(2,1)} async-done(((bf16[1024,1024]{1,0:T(8,128)(2,1)}), bf16[128,1024]{1,0:T(8,128)(2,1)}) %reduce-scatter.15.cloned.1.call-update) | async-done | bytes 262160
  439.1 46.3 %all-gather.11.cloned.1.call-done = bf16[1024,1024]{0,1:T(8,128)(2,1)} async-done(((bf16[128,1024]{0,1:T(8,128)(2,1)}), bf16[1024,1024]{0,1:T(8,128)(2,1)}) %all-gather.11.cloned.1.call-update) | async-done | bytes 2097168 | tf_op jit(solution)/shard_map/all_gather | solution.py:117
  485.5 1.7 broadcast.109
  487.1 18.8 %while.62 = (s32[]{:T(128)}, bf16[4,256,1024]{2,1,0:T(8,128)(2,1)}, s32[4]{0:T(128)S(1)}, bf16[1024,1024]{0,1:T(8,128)(2,1)}, bf16[8,2,128,128]{3,2,1,0:T(8,128)...) while((s32[]{:T(128)}, bf16[4,256,1024]{2,1,0:T(8,128)(2,1)}, ...), condition=%wide.region_15.17_spmd.clone, body=%wide.region_14.16_spmd.clone.sunk | while | flops 142606592 | bytes 6816483 | solution.py:22
  505.9 51.6 %while.65 = (s32[]{:T(128)}, f32[8,2,128,128]{3,2,1,0:T(8,128)}, f32[8,2,128,128]{2,3,1,0:T(8,128)}, bf16[1024,1024]{0,1:T(8,128)(2,1)}, s32[8,1,2]{2,0,1:T(8,12...) while((s32[]{:T(128)}, f32[8,2,128,128]{3,2,1,0:T(8,128)}, ...), condition=%wide.wide.region_18.21_spmd.clone, body=%wide.wide.region_17.20_spmd.clone.sunk | while | flops 270533760 | bytes 28316308 | solution.py:141
  506.0 2.1 constant_dynamic-slice_fusion.22
  509.1 2.1 constant_dynamic-slice_fusion.23
  513.5 2.6 fusion.105
  516.2 1.5 convolution_add_fusion.3
  517.6 2.1 constant_dynamic-slice_fusion.22
  520.8 2.1 constant_dynamic-slice_fusion.23
  525.2 3.0 fusion.105
  528.2 2.7 convolution_add_fusion.3
  530.9 2.1 constant_dynamic-slice_fusion.22
  534.1 2.1 constant_dynamic-slice_fusion.23
  538.5 3.0 fusion.105
  541.5 2.7 convolution_add_fusion.3
  544.2 2.1 constant_dynamic-slice_fusion.22
  547.4 2.1 constant_dynamic-slice_fusion.23
  551.8 3.0 fusion.105
  554.8 2.7 convolution_add_fusion.3
  557.5 2.4 multiply_reduce_fusion
  560.5 79.3 %psum.31 = f32[]{:T(128)} all-reduce(f32[]{:T(128)} %multiply_reduce_fusion), channel_id=1, replica_groups=mesh['wide'=32,'blk'=8] {'wide','blk'}, use_global_device_ids=true, to_apply=%region_20.23 | all-reduce | flops 1 | bytes 8 | tf_op jit(solution)/shard_map/psum | solution.py:144
  640.8 2.9 multiply_bitcast_fusion
  643.7 1.5 divide_convert_fusion
  (226 shorter events, 77.3 us)
Async XLA Ops:
  7.2 56.5 %all-gather.5.cloned.1.call-start = ((), (), s32[]{:S(2)}) async-start(), calls=%async_computation.4 | async-start | bytes 2162688 | tf_op jit(solution)/shard_map/all_gather | solution.py:59
  7.9 165.9 %reduce-scatter.13.cloned.1.call-start = ((), (), s32[]{:S(2)}) async-start(), calls=%async_computation.10 | async-start | bytes 2359296
  8.7 58.9 %copy-start.16 = (s32[8,1,2]{2,0,1:T(8,128)}, s32[8,1,2]{2,0,1:T(8,128)S(1)}, u32[]{:S(2)}) copy-start(s32[8,1,2]{2,0,1:T(8,128)S(1)} %copy.96) | copy-start | bytes 196
  11.6 57.5 %copy-start.5 = (bf16[8,2,128,128]{3,2,1,0:T(8,128)(2,1)}, bf16[8,2,128,128]{3,2,1,0:T(8,128)(2,1)S(1)}, u32[]{:S(2)}) copy-start(bf16[8,2,128,128]{3,2,1,0:T(8,128)(2,1)S(1)} %get-tuple-element.952) | copy-start | bytes 1572868
  73.3 1.0 copy-start.9
  73.6 1.6 copy-start.10
  75.3 1.4 copy-start.11
  80.9 1.0 copy-start.9
  81.2 1.6 copy-start.10
  82.9 1.4 copy-start.11
  88.2 0.7 copy-start.17
  88.2 0.8 copy-start.15
  88.2 0.9 copy-start.14
  88.2 2.1 copy-start.6
  88.3 126.8 %copy-start.1 = (bf16[8,2,128,128]{3,2,1,0:T(8,128)(2,1)S(1)}, bf16[8,2,128,128]{3,2,1,0:T(8,128)(2,1)}, u32[]{:S(2)}) copy-start(bf16[8,2,128,128]{3,2,1,0:T(8,128)(2,1)} %get-tuple-element.920) | copy-start | bytes 1572868
  88.3 125.1 %all-gather.7.cloned.1.call-start = ((), (), s32[]{:S(2)}) async-start(), calls=%async_computation.5 | async-start | bytes 2359296 | tf_op jit(solution)/shard_map/all_gather | solution.py:81
  175.9 145.3 %reduce-scatter.9.cloned.1.call-start = ((), (), s32[]{:S(2)}) async-start(), calls=%async_computation.6 | async-start | bytes 2162688 | tf_op jit(solution)/shard_map/reduce_scatter | solution.py:92
  233.3 87.9 %copy-start.19 = (bf16[32,1024]{1,0:T(8,128)(2,1)S(1)}, bf16[32,1024]{1,0:T(8,128)(2,1)}, u32[]{:S(2)}) copy-start(bf16[32,1024]{1,0:T(8,128)(2,1)} %param.22) | copy-start | bytes 196612
  233.4 141.2 %all-gather.9.cloned.1.call-start = ((), (), s32[]{:S(2)}) async-start(), calls=%async_computation.7 | async-start | bytes 2162688 | tf_op jit(solution)/shard_map/all_gather | solution.py:99
  322.8 113.8 %reduce-scatter.15.cloned.1.call-start = ((), (), s32[]{:S(2)}) async-start(), calls=%async_computation.11 | async-start | bytes 2359296
  380.0 2.6 copy-start.2
  384.3 1.0 copy-start.3
  384.6 1.6 copy-start.12
  386.3 1.4 copy-start.13
  387.7 2.6 copy-start.2
  392.0 1.0 copy-start.3
  392.3 1.6 copy-start.12
  394.1 1.4 copy-start.13
  399.5 39.6 %copy-start.18 = (s32[8,1,2]{2,0,1:T(8,128)S(1)}, s32[8,1,2]{2,0,1:T(8,128)}, u32[]{:S(2)}) copy-start(s32[8,1,2]{2,0,1:T(8,128)} %get-tuple-element.1050) | copy-start | bytes 196
  399.5 87.6 %copy-start.7 = (bf16[8,2,128,128]{3,2,1,0:T(8,128)(2,1)S(1)}, bf16[8,2,128,128]{3,2,1,0:T(8,128)(2,1)}, u32[]{:S(2)}) copy-start(bf16[8,2,128,128]{3,2,1,0:T(8,128)(2,1)} %copy-done.5) | copy-start | bytes 1572868
  399.5 86.0 %all-gather.11.cloned.1.call-start = ((), (), s32[]{:S(2)}) async-start(), calls=%async_computation.8 | async-start | bytes 2359296 | tf_op jit(solution)/shard_map/all_gather | solution.py:117
  438.8 204.9 %reduce-scatter.11.cloned.1.call-start = ((), (), s32[]{:S(2)}) async-start(), calls=%async_computation.9 | async-start | bytes 2162688 | tf_op jit(solution)/shard_map/reduce_scatter | solution.py:156
  513.5 2.6 copy-start
  513.5 2.6 copy-start.4
  525.2 3.0 copy-start
  525.2 3.0 copy-start.4
  538.5 3.0 copy-start
  538.5 3.0 copy-start.4
  551.8 3.0 copy-start
  551.8 3.0 copy-start.4
  557.5 82.3 %copy-start.8 = (f32[8,2,128,128]{2,3,1,0:T(8,128)S(1)}, f32[8,2,128,128]{2,3,1,0:T(8,128)}, u32[]{:S(2)}) copy-start(f32[8,2,128,128]{2,3,1,0:T(8,128)} %get-tuple-element.279) | copy-start | bytes 3145732
Sparse Core Ops, SparseCore 0:
  10.6 53.0 all-gather.4
  88.4 37.0 reduce-scatter.12
  176.0 37.3 all-gather.6
  233.5 87.7 reduce-scatter.8
  324.2 50.2 all-gather.8
  399.6 36.9 reduce-scatter.14
  438.9 46.4 all-gather.10
  506.1 87.7 reduce-scatter.10
where the time goes:
time: 654 us; the launch traced here: 652 us
  waiting for transfers between devices  312 us (48%)
  blocking collectives  161 us (25%)
  local copies, waits for them, and re-layouts  98.7 us (15%)
  matrix products  34 us (5%)
  other arithmetic  20.6 us (3%)
  between operations  16.8 us (3%)
  loops' own time  8.79 us (1%)
    reduce_scatter x1, waiting for transfers between devices, body(): lax.psum_scatter(by_blocks(output_block_term, owned * lax.axis_size('wide...  87.8 us
    psum x1, blocking collectives, body(): lax.psum(jnp.sum(raw_in * tiles_in.astype(jnp.float32)), ('wide', 'blk'))  79.3 us
    psum x1, blocking collectives, body(): norm_image = lax.psum(jnp.sum(image * image), 'wide')  65.7 us
    all_gather x1, waiting for transfers between devices, body(): error_full = lax.all_gather(residual, 'wide', axis=0, tiled=True)  51.6 us
    all_gather x1, waiting for transfers between devices, body(): x_full = lax.all_gather(tokens, 'wide', axis=0, tiled=True)  51 us
    all_gather x1, waiting for transfers between devices, body(): slope_full = lax.all_gather(slope_own, 'blk', axis=0, tiled=True)  46.3 us
    unnamed x10, waiting for transfers between devices  37.8 us
    all_gather x1, waiting for transfers between devices, body(): active_full = lax.all_gather(active_own, 'blk', axis=0, tiled=True)  37.4 us
  transfers between devices with their start and end apart: 8, of which 6 were waited for; matrix products, arithmetic and copies ran while one was open for 10% of the time, Pallas kernels for 0%

commit v1 on v0

--- a/solution.py
+++ b/solution.py
@@ -96,7 +96,11 @@
         tiled=True,
     )
     residual = (outputs.astype(jnp.float32) - target.astype(jnp.float32)).astype(jnp.bfloat16)
-    error_full = lax.all_gather(residual, "wide", axis=0, tiled=True)
+    count_2 = lax.axis_size("wide")
+    repeats = [count_2 if d == 0 else 1 for d in range(residual.ndim)]
+    error_full = lax.all_to_all(
+        jnp.tile(residual, repeats), "wide", split_axis=0, concat_axis=0, tiled=True
+    )
 
     def back_block_term(start_row, count):
         picked = pick_rows(

time: 654 us -> 636 us (0.972)
  waiting for transfers between devices: 312 us -> 287 us
  starting transfers between devices: 0.51 us -> 7.79 us
    all_gather x1 -> x0, waiting for transfers between devices: 51.6 us -> none  [body(): error_full = lax.all_gather(residual, 'wide', axis=0, tiled=True)]
    all_to_all x0 -> x1, waiting for transfers between devices: none -> 28.2 us  [body(): lax.all_to_all(jnp.tile(residual, repeats), 'wide', split_axis=0, concat_...]
    all_to_all x0 -> x1, starting transfers between devices: none -> 7.32 us  [body(): lax.all_to_all(jnp.tile(residual, repeats), 'wide', split_axis=0, concat_...]
    unnamed x10 -> x9, waiting for transfers between devices: 37.8 us -> 36.6 us
where the time goes in v1:
time: 636 us; the launch traced here: 634 us
  waiting for transfers between devices  287 us (45%)
  blocking collectives  161 us (25%)
  local copies, waits for them, and re-layouts  99.1 us (16%)
  matrix products  34 us (5%)
  other arithmetic  20 us (3%)
  between operations  16.9 us (3%)
  loops' own time  8.89 us (1%)
  starting transfers between devices  7.79 us (1%)
    reduce_scatter x1, waiting for transfers between devices, body(): lax.psum_scatter(by_blocks(output_block_term, owned * lax.axis_size('wide...  87.8 us
    psum x1, blocking collectives, body(): lax.psum(jnp.sum(raw_in * tiles_in.astype(jnp.float32)), ('wide', 'blk'))  79.3 us
    psum x1, blocking collectives, body(): norm_image = lax.psum(jnp.sum(image * image), 'wide')  65.7 us
    all_gather x1, waiting for transfers between devices, body(): x_full = lax.all_gather(tokens, 'wide', axis=0, tiled=True)  51 us
    all_gather x1, waiting for transfers between devices, body(): slope_full = lax.all_gather(slope_own, 'blk', axis=0, tiled=True)  46.2 us
    all_gather x1, waiting for transfers between devices, body(): active_full = lax.all_gather(active_own, 'blk', axis=0, tiled=True)  37.4 us
    unnamed x9, waiting for transfers between devices  36.6 us
    all_to_all x1, waiting for transfers between devices, body(): lax.all_to_all(jnp.tile(residual, repeats), 'wide', split_axis=0, concat_...  28.2 us
  transfers between devices with their start and end apart: 8, of which 6 were waited for; matrix products, arithmetic and copies ran while one was open for 10% of the time, Pallas kernels for 0%

profile of v1, /device:TPU:1, one launch (start us, length us, event | category | flops | bytes accessed | tf_op | source)
XLA Modules:
  0.0 634.5 jit_solution(1554174019944542009)
XLA Ops:
  9.5 2.1 bitcast_multiply_fusion
  12.7 51.0 %all-gather.4.cloned.1.call-done = bf16[1024,1024]{1,0:T(8,128)(2,1)} async-done(((bf16[32,1024]{1,0:T(8,128)(2,1)}), bf16[1024,1024]{1,0:T(8,128)(2,1)}) %all-gather.4.cloned.1.call-update) | async-done | bytes 2097168 | tf_op jit(solution)/shard_map/all_gather | solution.py:59
  63.7 3.9 copy.94
  67.6 1.5 broadcast.113.clone
  69.1 15.2 %while.63 = (s32[]{:T(128)}, bf16[2,512,1024]{1,2,0:T(8,128)(2,1)}, s32[2]{0:T(128)S(1)}, bf16[1024,1024]{0,1:T(8,128)(2,1)}, s32[8,1,2]{2,0,1:T(8,128)}, /*inde...) while((s32[]{:T(128)}, bf16[2,512,1024]{1,2,0:T(8,128)(2,1)}, ...), condition=%wide.wide.region_1.3_spmd, body=%wide.wide.region_0.0_spmd.sunk | while | flops 269485216 | bytes 37229152 | solution.py:22
  75.4 1.3 copy-done.11
  82.9 1.3 copy-done.11
  84.3 3.9 copy.131
  90.7 15.5 %all-reduce = (f32[8,128]{1,0:T(8,128)S(1)}, f32[]{:T(128)}) all-reduce(f32[8,128]{1,0:T(8,128)S(1)} %bitcast.246, f32[]{:T(128)} %multiply_reduce_fusion.1), channel_id=1, replica_groups=mesh['wide'=32,'blk'=8] {'blk'}, use_global_device_ids=true, to_apply=%region_3.5 | all-reduce | flops 1025 | bytes 8200 | tf_op jit(solution)/shard_map/psum | solution.py:56
  106.8 65.7 %psum.29 = f32[]{:T(128)} all-reduce(f32[]{:T(128)} %multiply_reduce_fusion.2), channel_id=1, replica_groups=mesh['wide'=32,'blk'=8] {'wide'}, use_global_device_ids=true, to_apply=%region_5.7 | all-reduce | flops 1 | bytes 8 | tf_op jit(solution)/shard_map/psum | solution.py:57
  176.0 37.4 %all-gather.6.cloned.1.call-done = bf16[1024,1024]{0,1:T(8,128)(2,1)} async-done(((bf16[128,1024]{0,1:T(8,128)(2,1)}), bf16[1024,1024]{0,1:T(8,128)(2,1)}) %all-gather.6.cloned.1.call-update) | async-done | bytes 2097168 | tf_op jit(solution)/shard_map/all_gather | solution.py:81
  213.5 1.6 broadcast.112.clone
  215.1 18.3 %while.61 = (s32[]{:T(128)}, bf16[4,256,1024]{2,1,0:T(8,128)(2,1)}, s32[4]{0:T(128)S(1)}, bf16[1024,1024]{0,1:T(8,128)(2,1)}, bf16[8,2,128,128]{3,2,1,0:T(8,128)...) while((s32[]{:T(128)}, bf16[4,256,1024]{2,1,0:T(8,128)(2,1)}, ...), condition=%wide.region_9.11_spmd.clone, body=%wide.region_8.10_spmd.clone.sunk | while | flops 142606592 | bytes 6816483 | solution.py:22
  233.4 87.8 %reduce-scatter.9.cloned.1.call-done = bf16[32,1024]{1,0:T(8,128)(2,1)} async-done(((bf16[1024,1024]{1,0:T(8,128)(2,1)}), bf16[32,1024]{1,0:T(8,128)(2,1)}) %reduce-scatter.9.cloned.1.call-update) | async-done | bytes 65552 | tf_op jit(solution)/shard_map/reduce_scatter | solution.py:92
  322.1 1.6 tile.2
  323.7 7.3 %all-to-all-start = ((bf16[32,32,1024]{2,1,0:T(8,128)(2,1)}), bf16[32,32,1024]{2,1,0:T(8,128)(2,1)S(1)}, u32[]{:S(2)}, u32[]{:S(2)}) async-start(bf16[32,32,1024]{2,1,0:T(8,128)(2,1)} %tile.2), calls=%async_computation.1 | async-start | bytes 4194304 | tf_op jit(solution)/shard_map/all_to_all | solution.py:101
  331.1 28.2 %all-to-all-done = bf16[32,32,1024]{2,1,0:T(8,128)(2,1)S(1)} async-done(((bf16[32,32,1024]{2,1,0:T(8,128)(2,1)}), bf16[32,32,1024]{2,1,0:T(8,128)(2,1)S(1)}, u32[]{:S(2)}, u32[]{:S(2)}) %all-to-all-start) | async-done | bytes 2097184 | tf_op jit(solution)/shard_map/all_to_all | solution.py:101
  359.3 2.6 copy.100
  361.9 1.5 broadcast.113
  363.4 15.7 %while.64 = (s32[]{:T(128)}, bf16[2,512,1024]{1,2,0:T(8,128)(2,1)}, s32[2]{0:T(128)S(1)}, bf16[1024,1024]{0,1:T(8,128)(2,1)}, s32[8,1,2]{2,0,1:T(8,128)}, /*inde...) while((s32[]{:T(128)}, bf16[2,512,1024]{1,2,0:T(8,128)(2,1)}, ...), condition=%wide.wide.region_12.14_spmd, body=%wide.wide.region_11.13_spmd.sunk | while | flops 269485216 | bytes 39326336 | solution.py:22
  369.9 1.4 copy-done.13
  377.7 1.4 copy-done.13
  379.1 4.0 copy.132
  383.2 35.8 %reduce-scatter.15.cloned.1.call-done = bf16[128,1024]{1,0:T(8,128)(2,1)} async-done(((bf16[1024,1024]{1,0:T(8,128)(2,1)}), bf16[128,1024]{1,0:T(8,128)(2,1)}) %reduce-scatter.15.cloned.1.call-update) | async-done | bytes 262160
  421.5 46.2 %all-gather.8.cloned.1.call-done = bf16[1024,1024]{0,1:T(8,128)(2,1)} async-done(((bf16[128,1024]{0,1:T(8,128)(2,1)}), bf16[1024,1024]{0,1:T(8,128)(2,1)}) %all-gather.8.cloned.1.call-update) | async-done | bytes 2097168 | tf_op jit(solution)/shard_map/all_gather | solution.py:121
  467.7 1.7 broadcast.112
  469.4 18.9 %while.62 = (s32[]{:T(128)}, bf16[4,256,1024]{2,1,0:T(8,128)(2,1)}, s32[4]{0:T(128)S(1)}, bf16[1024,1024]{0,1:T(8,128)(2,1)}, bf16[8,2,128,128]{3,2,1,0:T(8,128)...) while((s32[]{:T(128)}, bf16[4,256,1024]{2,1,0:T(8,128)(2,1)}, ...), condition=%wide.region_15.17_spmd.clone, body=%wide.region_14.16_spmd.clone.sunk | while | flops 142606592 | bytes 6816483 | solution.py:22
  488.3 51.6 %while.65 = (s32[]{:T(128)}, f32[8,2,128,128]{3,2,1,0:T(8,128)}, f32[8,2,128,128]{2,3,1,0:T(8,128)}, bf16[1024,1024]{0,1:T(8,128)(2,1)}, s32[8,1,2]{2,0,1:T(8,12...) while((s32[]{:T(128)}, f32[8,2,128,128]{3,2,1,0:T(8,128)}, ...), condition=%wide.wide.region_18.21_spmd.clone, body=%wide.wide.region_17.20_spmd.clone.sunk | while | flops 270533760 | bytes 28316308 | solution.py:145
  488.3 2.1 constant_dynamic-slice_fusion.22
  491.5 2.1 constant_dynamic-slice_fusion.23
  495.9 2.6 fusion.105
  498.5 1.5 convolution_add_fusion.3
  500.0 2.1 constant_dynamic-slice_fusion.22
  503.2 2.1 constant_dynamic-slice_fusion.23
  507.6 3.0 fusion.105
  510.6 2.7 convolution_add_fusion.3
  513.3 2.1 constant_dynamic-slice_fusion.22
  516.5 2.1 constant_dynamic-slice_fusion.23
  520.9 3.0 fusion.105
  523.9 2.7 convolution_add_fusion.3
  526.6 2.2 constant_dynamic-slice_fusion.22
  529.8 2.1 constant_dynamic-slice_fusion.23
  534.2 3.0 fusion.105
  537.2 2.7 convolution_add_fusion.3
  539.9 2.4 multiply_reduce_fusion
  542.9 79.3 %psum.31 = f32[]{:T(128)} all-reduce(f32[]{:T(128)} %multiply_reduce_fusion), channel_id=1, replica_groups=mesh['wide'=32,'blk'=8] {'wide','blk'}, use_global_device_ids=true, to_apply=%region_20.23 | all-reduce | flops 1 | bytes 8 | tf_op jit(solution)/shard_map/psum | solution.py:148
  623.2 2.9 multiply_bitcast_fusion
  626.2 1.5 divide_convert_fusion
  (226 shorter events, 79.6 us)
Async XLA Ops:
  7.2 56.5 %all-gather.4.cloned.1.call-start = ((), (), s32[]{:S(2)}) async-start(), calls=%async_computation.5 | async-start | bytes 2162688 | tf_op jit(solution)/shard_map/all_gather | solution.py:59
  7.9 166.0 %reduce-scatter.13.cloned.1.call-start = ((), (), s32[]{:S(2)}) async-start(), calls=%async_computation.10 | async-start | bytes 2359296
  8.7 58.9 %copy-start.16 = (s32[8,1,2]{2,0,1:T(8,128)}, s32[8,1,2]{2,0,1:T(8,128)S(1)}, u32[]{:S(2)}) copy-start(s32[8,1,2]{2,0,1:T(8,128)S(1)} %copy.95) | copy-start | bytes 196
  11.6 57.4 %copy-start.5 = (bf16[8,2,128,128]{3,2,1,0:T(8,128)(2,1)}, bf16[8,2,128,128]{3,2,1,0:T(8,128)(2,1)S(1)}, u32[]{:S(2)}) copy-start(bf16[8,2,128,128]{3,2,1,0:T(8,128)(2,1)S(1)} %get-tuple-element.952) | copy-start | bytes 1572868
  73.3 1.0 copy-start.9
  73.6 1.6 copy-start.10
  75.3 1.3 copy-start.11
  80.9 1.0 copy-start.9
  81.2 1.6 copy-start.10
  82.9 1.3 copy-start.11
  88.2 0.7 copy-start.17
  88.2 0.8 copy-start.15
  88.2 0.9 copy-start.14
  88.2 2.1 copy-start.6
  88.3 126.8 %copy-start.1 = (bf16[8,2,128,128]{3,2,1,0:T(8,128)(2,1)S(1)}, bf16[8,2,128,128]{3,2,1,0:T(8,128)(2,1)}, u32[]{:S(2)}) copy-start(bf16[8,2,128,128]{3,2,1,0:T(8,128)(2,1)} %get-tuple-element.920) | copy-start | bytes 1572868
  88.3 125.2 %all-gather.6.cloned.1.call-start = ((), (), s32[]{:S(2)}) async-start(), calls=%async_computation.6 | async-start | bytes 2359296 | tf_op jit(solution)/shard_map/all_gather | solution.py:81
  176.0 145.2 %reduce-scatter.9.cloned.1.call-start = ((), (), s32[]{:S(2)}) async-start(), calls=%async_computation.7 | async-start | bytes 2162688 | tf_op jit(solution)/shard_map/reduce_scatter | solution.py:92
  233.4 87.8 %copy-start.19 = (bf16[32,1024]{1,0:T(8,128)(2,1)S(1)}, bf16[32,1024]{1,0:T(8,128)(2,1)}, u32[]{:S(2)}) copy-start(bf16[32,1024]{1,0:T(8,128)(2,1)} %param.22) | copy-start | bytes 196612
  323.7 35.6 %all-to-all-start = ((bf16[32,32,1024]{2,1,0:T(8,128)(2,1)}), bf16[32,32,1024]{2,1,0:T(8,128)(2,1)S(1)}, u32[]{:S(2)}, u32[]{:S(2)}) async-start(bf16[32,32,1024]{2,1,0:T(8,128)(2,1)} %tile.2), calls=%async_computation.1 | async-start | bytes 4194304 | tf_op jit(solution)/shard_map/all_to_all | solution.py:101
  331.0 87.9 %reduce-scatter.15.cloned.1.call-start = ((), (), s32[]{:S(2)}) async-start(), calls=%async_computation.11 | async-start | bytes 2359296
  363.4 2.7 copy-start.2
  367.8 1.0 copy-start.3
  368.1 1.6 copy-start.12
  369.8 1.4 copy-start.13
  371.2 2.7 copy-start.2
  375.7 1.0 copy-start.3
  375.9 1.6 copy-start.12
  377.7 1.4 copy-start.13
  383.1 38.3 %copy-start.18 = (s32[8,1,2]{2,0,1:T(8,128)S(1)}, s32[8,1,2]{2,0,1:T(8,128)}, u32[]{:S(2)}) copy-start(s32[8,1,2]{2,0,1:T(8,128)} %get-tuple-element.1049) | copy-start | bytes 196
  383.1 86.3 %copy-start.7 = (bf16[8,2,128,128]{3,2,1,0:T(8,128)(2,1)S(1)}, bf16[8,2,128,128]{3,2,1,0:T(8,128)(2,1)}, u32[]{:S(2)}) copy-start(bf16[8,2,128,128]{3,2,1,0:T(8,128)(2,1)} %copy-done.5) | copy-start | bytes 1572868
  383.1 84.6 %all-gather.8.cloned.1.call-start = ((), (), s32[]{:S(2)}) async-start(), calls=%async_computation.8 | async-start | bytes 2359296 | tf_op jit(solution)/shard_map/all_gather | solution.py:121
  421.2 205.0 %reduce-scatter.11.cloned.1.call-start = ((), (), s32[]{:S(2)}) async-start(), calls=%async_computation.9 | async-start | bytes 2162688 | tf_op jit(solution)/shard_map/reduce_scatter | solution.py:160
  495.9 2.6 copy-start
  495.9 2.6 copy-start.4
  507.6 3.0 copy-start
  507.6 3.0 copy-start.4
  520.9 3.0 copy-start
  520.9 3.0 copy-start.4
  534.2 3.0 copy-start
  534.2 3.0 copy-start.4
  539.9 82.4 %copy-start.8 = (f32[8,2,128,128]{2,3,1,0:T(8,128)S(1)}, f32[8,2,128,128]{2,3,1,0:T(8,128)}, u32[]{:S(2)}) copy-start(f32[8,2,128,128]{2,3,1,0:T(8,128)} %get-tuple-element.279) | copy-start | bytes 3145732
Sparse Core Ops, SparseCore 0:
  10.6 53.0 all-gather.3
  88.4 37.0 reduce-scatter.12
  176.1 37.3 all-gather.5
  233.5 87.6 reduce-scatter.8
  383.2 35.6 reduce-scatter.14
  421.3 46.3 all-gather.7
  488.4 87.8 reduce-scatter.10
